TPU v7x, 512 devices: a whole 4x8x8 slice. The times are simulated.
512 devices in a mesh: group: 32 (over y, x), member: 16 (over z, core).
Axes of the slice: x: 4, y: 8, z: 8, core: 2. Of those that a mesh axis runs over, the one named last changes fastest.
Arguments:
- feats: bfloat16 [262144, 1024], P(('group', 'member')), may hold values from -24 to 24
- transform: bfloat16 [1024, 1024], replicated, may hold values from -0.1875 to 0.1875
- bias: float32 [1024], replicated, may hold values from -3 to 3
- tile_list: int32 [2048, 8], P(('group', 'member')), may hold values from 0 to 255, as said below
- nbr_slot: int32 [262144, 16], P(('group', 'member')), may hold values from 0 to 255
- nbr_weight: int32 [262144, 16], P(('group', 'member')), may hold values from 1 to 16
- cotangent: bfloat16 [262144, 1024], P(('group', 'member')), may hold values from -6 to 6
Outputs:
- embedding: bfloat16 [262144, 1024], P(('group', 'member'))
- feat_grad: bfloat16 [262144, 1024], P(('group', 'member'))
- transform_grad: float32 [1024, 1024], P('member')
Inputs may be any that keep to these rules, and one draw needn't show every extreme that they name: `tile_list`: each block lists 8 different tiles of its own group; group tile g lies on member g // 16 of that group. Over all blocks of one device, the tiles that lie on another member are at most one distinct tile for each such member.
All inputs are finite; a program needn't handle non-finite values.
Results may differ from a plain program's by a relative error of at most 0.013.
Values may be sent and summed in bfloat16 or wider, within the bound.
No kernel may reach another device: no remote copies, remote signals or barrier semaphores. Data moves between devices by JAX's collectives and lax.ppermute only.
A program may use at most 64 MiB of HBM per device.

v0:
```python
import math
import jax
import jax.numpy as jnp
from jax import lax
from jax.sharding import PartitionSpec as P

TILE = 32


def adjacency_of(slot_rows, weights, cand_width):
    columns = lax.broadcasted_iota(jnp.int32, slot_rows.shape + (cand_width,), slot_rows.ndim)
    matched_weights = jnp.where(slot_rows[..., None] == columns, weights[..., None], 0)
    return jnp.sum(matched_weights, axis=-2).astype(jnp.bfloat16)


def on_device(feats, transform, bias, tile_list, nbr_slot, nbr_weight, cotangent):
    rows_dev, feat_width = feats.shape
    hidden_width = transform.shape[1]
    blocks, tiles_per = tile_list.shape
    block_rows = rows_dev // blocks
    members = lax.axis_size("member")
    groups = lax.axis_size("group")
    member_here = lax.axis_index("member")
    tiles_dev = rows_dev // TILE
    cand_width = tiles_per * TILE
    preact = jnp.dot(feats, transform, preferred_element_type=jnp.float32) + bias
    message = jnp.maximum(preact, 0.0).astype(jnp.bfloat16)
    own_tiles = message.reshape(tiles_dev, TILE, hidden_width)
    holder = tile_list // tiles_dev
    local_index = tile_list % tiles_dev
    foreign = holder != member_here
    peer_ids = lax.broadcasted_iota(jnp.int32, (1, 1, members), 2)
    matched = (holder[..., None] == peer_ids) & foreign[..., None]
    wanted = jnp.max(jnp.where(matched, local_index[..., None], -1), axis=(0, 1))
    asked_for = lax.all_to_all(
        wanted.reshape(members, 1), "member", split_axis=0, concat_axis=0, tiled=True
    )[:, 0]
    served = jnp.clip(asked_for, 0, tiles_dev - 1)
    remote = lax.all_to_all(own_tiles[served], "member", split_axis=0, concat_axis=0, tiled=True)
    tile_pool = jnp.concatenate([remote, own_tiles], axis=0)
    pool_index = jnp.where(foreign, holder, members + local_index).reshape(-1)
    candidates = tile_pool[pool_index].reshape(blocks, cand_width, hidden_width)
    slot_rows = nbr_slot.reshape(blocks, block_rows, -1)
    weights = nbr_weight.reshape(blocks, block_rows, -1)
    adjacency = adjacency_of(slot_rows, weights, cand_width)
    weight_total = jnp.sum(weights, axis=2).astype(jnp.float32)[..., None]
    gathered = jnp.einsum("brc,bch->brh", adjacency, candidates, preferred_element_type=jnp.float32)
    combined = gathered / weight_total + message.reshape(blocks, block_rows, hidden_width).astype(
        jnp.float32
    )
    inv_rms = lax.rsqrt(jnp.mean(combined * combined, axis=2, keepdims=True) + 1e-06)
    normed = combined * inv_rms
    embedding = normed.astype(jnp.bfloat16).reshape(rows_dev, hidden_width)
    incoming = cotangent.reshape(blocks, block_rows, hidden_width).astype(jnp.float32)
    mixed_grad = inv_rms * (incoming - normed * jnp.mean(incoming * normed, axis=2, keepdims=True))
    agg_grad = (mixed_grad / weight_total).astype(jnp.bfloat16)
    cand_grad = jnp.einsum("brc,brh->bch", adjacency, agg_grad, preferred_element_type=jnp.float32)
    cand_grad = cand_grad.reshape(blocks * tiles_per, TILE, hidden_width)
    pool_size = members + tiles_dev
    pool_grad = jax.ops.segment_sum(cand_grad, pool_index, num_segments=pool_size)
    returned = pool_grad[:members].astype(jnp.bfloat16)
    came_back = lax.all_to_all(returned, "member", split_axis=0, concat_axis=0, tiled=True)
    back_rows = jnp.where((asked_for >= 0)[:, None, None], came_back.astype(jnp.float32), 0.0)
    tile_grad = pool_grad[members:].at[served].add(back_rows)
    message_grad = mixed_grad.reshape(rows_dev, hidden_width) + tile_grad.reshape(
        rows_dev, hidden_width
    )
    pre_grad = jnp.where(preact > 0, message_grad, 0.0).astype(jnp.bfloat16)
    feat_grad = lax.dot_general(
        pre_grad, transform, (((1,), (1,)), ((), ())), preferred_element_type=jnp.float32
    ).astype(jnp.bfloat16)
    row_share = lax.psum_scatter(
        lax.dot_general(
            feats, pre_grad, (((0,), (0,)), ((), ())), preferred_element_type=jnp.float32
        ),
        "member",
        scatter_dimension=0,
        tiled=True,
    )
    factor = 1.0 / math.sqrt(rows_dev * members * groups)
    transform_grad = lax.psum(row_share, "group") * factor
    return (embedding, feat_grad, transform_grad)


def solution(mesh):
    return jax.shard_map(
        on_device,
        mesh=mesh,
        in_specs=(
            P(("group", "member"), None),
            P(),
            P(),
            P(("group", "member"), None),
            P(("group", "member"), None),
            P(("group", "member"), None),
            P(("group", "member"), None),
        ),
        out_specs=(P(("group", "member"), None), P(("group", "member"), None), P("member", None)),
        check_vma=False,
    )
```

profile of v0, /device:TPU:64, one launch (start us, length us, event | category | flops | bytes accessed | tf_op | source)
XLA Modules:
  0.0 374.1 jit_solution(13772715015103534861)
XLA Ops:
  8.8 10.0 %all-to-all-start = ((s32[16,1,1]{2,1,0:T(1,128)}), s32[16,1,1]{2,1,0:T(1,128)S(1)}, u32[]{:S(2)}, u32[]{:S(2)}) async-start(s32[16,1,1]{2,1,0:T(1,128)} %copy.26), calls=%async_computation | async-start | bytes 16384 | tf_op jit(solution)/shard_map/all_to_all | solution.py:35
  18.8 3.9 %maximum_convert_fusion = (bf16[512,1024]{1,0:T(8,128)(2,1)S(1)}, f32[512,1024]{1,0:T(8,128)}) fusion(f32[1024]{0:T(1024)} %param.9, bf16[512,1024]{1,0:T(8,128)(2,1)} %param.7, bf16[1024,1024]{1,0:T(8,128)(2,1)S(1)} %copy-done), kind=kOutput, calls=%fused_computation.20 | convolution fusion | flops 1075314688 | bytes 6295552 | tf_op jit(solution)/shard_map/dot_general | solution.py:26
  22.7 2.3 all-to-all-done
  27.0 5.5 %all-to-all-start.1 = ((bf16[16,32,1024]{2,1,0:T(8,128)(2,1)}), bf16[16,32,1024]{2,1,0:T(8,128)(2,1)}, u32[]{:S(2)}, u32[]{:S(2)}) async-start(bf16[16,32,1024]{2,1,0:T(8,128)(2,1)} %gather_fusion), calls=%async_computation.1 | async-start | bytes 2097152 | tf_op jit(solution)/shard_map/all_to_all | solution.py:39
  33.7 5.9 %select_reduce_fusion = s32[4,128,256]{2,1,0:T(8,128)} fusion(s32[4,128,16]{2,1,0:T(8,128)S(1)} %bitcast.44, s32[4,128,16]{2,1,0:T(8,128)} %bitcast.45), kind=kLoop, calls=%fused_computation.4 | loop fusion | flops 6160384 | bytes 589824 | tf_op jit(solution)/shard_map/reduce_sum | solution.py:13
  39.6 17.6 %all-to-all-done.1 = bf16[16,32,1024]{2,1,0:T(8,128)(2,1)} async-done(((bf16[16,32,1024]{2,1,0:T(8,128)(2,1)}), bf16[16,32,1024]{2,1,0:T(8,128)(2,1)}, u32[]{:S(2)}, u32[]{:S(2)}) %all-to-all-start.1) | async-done | bytes 1048608 | tf_op jit(solution)/shard_map/all_to_all | solution.py:39
  57.3 2.8 pad_maximum_fusion
  60.0 3.6 gather_fusion.1
  63.6 2.6 multiply_reduce_fusion
  68.0 2.8 fusion.4
  70.8 2.5 broadcast_in_dim.61
  73.3 9.9 %scatter_fusion = f32[32,32,1024]{2,1,0:T(8,128)} fusion(f32[32,32,1024]{2,1,0:T(8,128)} %broadcast_in_dim.61, s32[32]{0:T(128)S(1)} %reshape.142, f32[32,32,1024]{2,1,0:T(8,128)} %bitcast.38), kind=kCustom, calls=%fused_computation.2 | custom fusion | flops 1048576 | bytes 12583040 | tf_op jit(solution)/shard_map/scatter-add | solution.py:60
  83.2 2.7 slice.16
  85.9 6.9 %all-to-all-start.2 = ((bf16[16,32,1024]{2,1,0:T(8,128)(2,1)}), bf16[16,32,1024]{2,1,0:T(8,128)(2,1)S(1)}, u32[]{:S(2)}, u32[]{:S(2)}) async-start(bf16[16,32,1024]{2,1,0:T(8,128)(2,1)} %slice.16), calls=%async_computation.2 | async-start | bytes 2097152 | tf_op jit(solution)/shard_map/all_to_all | solution.py:62
  93.3 3.2 slice.13
  96.4 21.0 %all-to-all-done.2 = bf16[16,32,1024]{2,1,0:T(8,128)(2,1)S(1)} async-done(((bf16[16,32,1024]{2,1,0:T(8,128)(2,1)}), bf16[16,32,1024]{2,1,0:T(8,128)(2,1)S(1)}, u32[]{:S(2)}, u32[]{:S(2)}) %all-to-all-start.2) | async-done | bytes 1048608 | tf_op jit(solution)/shard_map/all_to_all | solution.py:62
  119.2 5.1 %scatter_fusion.1 = f32[16,32,1024]{2,1,0:T(8,128)} fusion(f32[16,32,1024]{2,1,0:T(8,128)} %slice.13, s32[16]{0:T(128)S(1)} %fusion.10, f32[16,32,1024]{2,1,0:T(8,128)} %convert_select_fusion), kind=kCustom, calls=%fused_computation.3 | custom fusion | flops 524288 | bytes 6291520 | tf_op jit(solution)/shard_map/scatter-add | solution.py:64
  124.2 3.7 fusion.3
  128.0 3.3 convolution_bitcast_fusion
  131.2 5.3 %copy.32 = f32[1024,1024]{1,0:T(8,128)} copy(f32[1024,1024]{0,1:T(8,128)} %convolution_bitcast_fusion) | data formatting | bytes 8388608
  136.6 64.3 %reduce-scatter.4.cloned.1.call-done = f32[64,1024]{1,0:T(8,128)} async-done(((f32[1024,1024]{1,0:T(8,128)}), f32[64,1024]{1,0:T(8,128)}) %reduce-scatter.4.cloned.1.call-update) | async-done | bytes 262160
  201.0 1.9 copy.33
  203.0 2.3 convolution_convert_fusion
  205.2 160.1 %all-reduce.2.cloned.1.call-done = f32[64,1024]{0,1:T(8,128)} async-done(((f32[64,1024]{0,1:T(8,128)}), f32[64,1024]{0,1:T(8,128)}) %all-reduce.2.cloned.1.call-update) | async-done | bytes 262160 | tf_op jit(solution)/shard_map/psum | solution.py:81
  (44 shorter events, 10.8 us)
Async XLA Ops:
  7.2 11.6 %copy-start = (bf16[1024,1024]{1,0:T(8,128)(2,1)S(1)}, bf16[1024,1024]{1,0:T(8,128)(2,1)}, u32[]{:S(2)}) copy-start(bf16[1024,1024]{1,0:T(8,128)(2,1)} %param.8) | copy-start | bytes 6291460
  8.8 16.1 %all-to-all-start = ((s32[16,1,1]{2,1,0:T(1,128)}), s32[16,1,1]{2,1,0:T(1,128)S(1)}, u32[]{:S(2)}, u32[]{:S(2)}) async-start(s32[16,1,1]{2,1,0:T(1,128)} %copy.26), calls=%async_computation | async-start | bytes 16384 | tf_op jit(solution)/shard_map/all_to_all | solution.py:35
  25.4 7.3 %copy-start.5 = (s32[512,16]{0,1:T(8,128)S(1)}, s32[512,16]{0,1:T(8,128)}, u32[]{:S(2)}) copy-start(s32[512,16]{0,1:T(8,128)} %param.12) | copy-start | bytes 98308
  25.4 7.5 %copy-start.6 = (s32[512,16]{0,1:T(8,128)S(1)}, s32[512,16]{0,1:T(8,128)}, u32[]{:S(2)}) copy-start(s32[512,16]{0,1:T(8,128)} %param.11) | copy-start | bytes 98308
  27.0 30.3 %all-to-all-start.1 = ((bf16[16,32,1024]{2,1,0:T(8,128)(2,1)}), bf16[16,32,1024]{2,1,0:T(8,128)(2,1)}, u32[]{:S(2)}, u32[]{:S(2)}) async-start(bf16[16,32,1024]{2,1,0:T(8,128)(2,1)} %gather_fusion), calls=%async_computation.1 | async-start | bytes 2097152 | tf_op jit(solution)/shard_map/all_to_all | solution.py:39
  63.6 2.6 copy-start.2
  66.6 1.4 copy-start.4
  68.0 2.8 copy-start.1
  85.9 31.6 %all-to-all-start.2 = ((bf16[16,32,1024]{2,1,0:T(8,128)(2,1)}), bf16[16,32,1024]{2,1,0:T(8,128)(2,1)S(1)}, u32[]{:S(2)}, u32[]{:S(2)}) async-start(bf16[16,32,1024]{2,1,0:T(8,128)(2,1)} %slice.16), calls=%async_computation.2 | async-start | bytes 2097152 | tf_op jit(solution)/shard_map/all_to_all | solution.py:62
  92.8 108.1 %reduce-scatter.4.cloned.1.call-start = ((), (), s32[]{:S(2)}) async-start(), calls=%async_computation.5 | async-start | bytes 4456448
  119.2 5.1 %copy-start.7 = (f32[1024]{0:T(1024)S(1)}, f32[1024]{0:T(1024)}, u32[]{:S(2)}) copy-start(f32[1024]{0:T(1024)} %param.9) | copy-start | bytes 12292
  124.2 3.7 copy-start.3
  136.6 228.7 %all-reduce.2.cloned.1.call-start = ((), (), s32[]{:S(2)}) async-start(), calls=%async_computation.4 | async-start | bytes 1048576 | tf_op jit(solution)/shard_map/psum | solution.py:81
Sparse Core Ops, SparseCore 0:
  136.7 64.2 reduce-scatter.3
  204.4 160.8 all-reduce.1
where the time goes:
time: 375 us; the launch traced here: 374 us
  waiting for transfers between devices  265 us (71%)
  other arithmetic  33.8 us (9%)
  local copies, waits for them, and re-layouts  23.5 us (6%)
  starting transfers between devices  22.5 us (6%)
  matrix products  14.7 us (4%)
  between operations  14.2 us (4%)
    psum x1, waiting for transfers between devices, on_device(): transform_grad = lax.psum(row_share, 'group') * factor  160 us
    unnamed x3, waiting for transfers between devices  64.4 us
    all_to_all x1, waiting for transfers between devices, on_device(): lax.all_to_all(returned, 'member', split_axis=0, concat_axis=0, tiled=True)  21 us
    all_to_all x1, waiting for transfers between devices, on_device(): lax.all_to_all(own_tiles[served], 'member', split_axis=0, concat_axis=0,...  17.6 us
    all_to_all x1, starting transfers between devices, on_device(): lax.all_to_all(wanted.reshape(members, 1), 'member', split_axis=0, concat...  9.98 us
    scatter-add x1, other arithmetic, on_device(): jax.ops.segment_sum(cand_grad, pool_index, num_segments=pool_size)  9.92 us
    unnamed x19, local copies, waits for them, and re-layouts  8.22 us
  transfers between devices with their start and end apart: 5, of which 5 were waited for; matrix products, arithmetic and copies ran while one was open for 4% of the time, Pallas kernels for 0%

commit v1 on v0

--- a/solution.py
+++ b/solution.py
@@ -78,7 +78,7 @@
         tiled=True,
     )
     factor = 1.0 / math.sqrt(rows_dev * members * groups)
-    transform_grad = lax.psum(row_share, "group") * factor
+    transform_grad = jnp.sum(lax.all_gather(row_share, "group"), axis=0) * factor
     return (embedding, feat_grad, transform_grad)
 
 

time: 375 us -> 322 us (0.86)
  the two profiles are of different devices: /device:TPU:64 before, /device:TPU:1 now
where the time goes in v1:
time: 322 us; the launch traced here: 321 us
  waiting for transfers between devices  213 us (66%)
  other arithmetic  37.5 us (12%)
  local copies, waits for them, and re-layouts  20.7 us (6%)
  starting transfers between devices  20.2 us (6%)
  matrix products  14.7 us (5%)
  between operations  14.2 us (4%)
    all_gather x1, waiting for transfers between devices, on_device(): lax.all_gather(row_share, 'group')  104 us
    reduce_scatter x1, waiting for transfers between devices, on_device(): lax.psum_scatter(lax.dot_general(feats, pre_grad, (((0,), (0,)), ((), ())...  61.1 us
    all_to_all x1, waiting for transfers between devices, on_device(): lax.all_to_all(returned, 'member', split_axis=0, concat_axis=0, tiled=True)  24.3 us
    all_to_all x1, waiting for transfers between devices, on_device(): lax.all_to_all(own_tiles[served], 'member', split_axis=0, concat_axis=0,...  21 us
    all_to_all x1, starting transfers between devices, on_device(): lax.all_to_all(wanted.reshape(members, 1), 'member', split_axis=0, concat...  11.8 us
    scatter-add x1, other arithmetic, on_device(): jax.ops.segment_sum(cand_grad, pool_index, num_segments=pool_size)  9.99 us
  transfers between devices with their start and end apart: 5, of which 5 were waited for; matrix products, arithmetic and copies ran while one was open for 5% of the time, Pallas kernels for 0%

profile of v1, /device:TPU:1, one launch (start us, length us, event | category | flops | bytes accessed | tf_op | source)
XLA Modules:
  0.0 320.6 jit_solution(3301975225639665460)
XLA Ops:
  8.8 11.8 %all-to-all-start = ((s32[16,1,1]{2,1,0:T(1,128)}), s32[16,1,1]{2,1,0:T(1,128)S(1)}, u32[]{:S(2)}, u32[]{:S(2)}) async-start(s32[16,1,1]{2,1,0:T(1,128)} %copy.29), calls=%async_computation | async-start | bytes 16384 | tf_op jit(solution)/shard_map/all_to_all | solution.py:35
  20.6 3.9 %maximum_convert_fusion = (bf16[512,1024]{1,0:T(8,128)(2,1)S(1)}, f32[512,1024]{1,0:T(8,128)}) fusion(f32[1024]{0:T(1024)} %param.9, bf16[512,1024]{1,0:T(8,128)(2,1)} %param.7, bf16[1024,1024]{1,0:T(8,128)(2,1)S(1)} %copy-done), kind=kOutput, calls=%fused_computation.20 | convolution fusion | flops 1075314688 | bytes 6295552 | tf_op jit(solution)/shard_map/dot_general | solution.py:26
  24.5 3.1 all-to-all-done
  29.6 4.7 %all-to-all-start.1 = ((bf16[16,32,1024]{2,1,0:T(8,128)(2,1)}), bf16[16,32,1024]{2,1,0:T(8,128)(2,1)}, u32[]{:S(2)}, u32[]{:S(2)}) async-start(bf16[16,32,1024]{2,1,0:T(8,128)(2,1)} %gather_fusion), calls=%async_computation.1 | async-start | bytes 2097152 | tf_op jit(solution)/shard_map/all_to_all | solution.py:39
  35.5 5.9 %select_reduce_fusion = s32[4,128,256]{2,1,0:T(8,128)} fusion(s32[4,128,16]{2,1,0:T(8,128)S(1)} %bitcast.46, s32[4,128,16]{2,1,0:T(8,128)} %bitcast.47), kind=kLoop, calls=%fused_computation.4 | loop fusion | flops 6160384 | bytes 589824 | tf_op jit(solution)/shard_map/reduce_sum | solution.py:13
  41.5 21.0 %all-to-all-done.1 = bf16[16,32,1024]{2,1,0:T(8,128)(2,1)} async-done(((bf16[16,32,1024]{2,1,0:T(8,128)(2,1)}), bf16[16,32,1024]{2,1,0:T(8,128)(2,1)}, u32[]{:S(2)}, u32[]{:S(2)}) %all-to-all-start.1) | async-done | bytes 1048608 | tf_op jit(solution)/shard_map/all_to_all | solution.py:39
  62.5 2.8 pad_maximum_fusion
  65.2 3.6 %gather_fusion.1 = bf16[32,32,1024]{2,1,0:T(8,128)(2,1)} fusion(bf16[32,32,1024]{2,1,0:T(8,128)(2,1)} %pad_maximum_fusion, s32[1024]{0:T(1024)S(1)} %pad_clamp_fusion), kind=kCustom, calls=%fused_computation.1 | custom fusion | bytes 4194432 | tf_op jit(solution)/shard_map/gather | solution.py:42
  68.8 2.6 multiply_reduce_fusion
  73.3 2.8 fusion.4
  76.0 2.5 broadcast_in_dim.61
  78.5 10.0 %scatter_fusion = f32[32,32,1024]{2,1,0:T(8,128)} fusion(f32[32,32,1024]{2,1,0:T(8,128)} %broadcast_in_dim.61, s32[32]{0:T(128)S(1)} %reshape.142, f32[32,32,1024]{2,1,0:T(8,128)} %bitcast.40), kind=kCustom, calls=%fused_computation.2 | custom fusion | flops 1048576 | bytes 12583040 | tf_op jit(solution)/shard_map/scatter-add | solution.py:60
  88.5 2.7 slice.16
  91.2 3.6 %all-to-all-start.2 = ((bf16[16,32,1024]{2,1,0:T(8,128)(2,1)}), bf16[16,32,1024]{2,1,0:T(8,128)(2,1)S(1)}, u32[]{:S(2)}, u32[]{:S(2)}) async-start(bf16[16,32,1024]{2,1,0:T(8,128)(2,1)} %slice.16), calls=%async_computation.2 | async-start | bytes 2097152 | tf_op jit(solution)/shard_map/all_to_all | solution.py:62
  95.2 3.2 slice.13
  98.4 24.3 %all-to-all-done.2 = bf16[16,32,1024]{2,1,0:T(8,128)(2,1)S(1)} async-done(((bf16[16,32,1024]{2,1,0:T(8,128)(2,1)}), bf16[16,32,1024]{2,1,0:T(8,128)(2,1)S(1)}, u32[]{:S(2)}, u32[]{:S(2)}) %all-to-all-start.2) | async-done | bytes 1048608 | tf_op jit(solution)/shard_map/all_to_all | solution.py:62
  124.4 5.1 %scatter_fusion.1 = f32[16,32,1024]{2,1,0:T(8,128)} fusion(f32[16,32,1024]{2,1,0:T(8,128)} %slice.13, s32[16]{0:T(128)S(1)} %fusion.10, f32[16,32,1024]{2,1,0:T(8,128)} %convert_select_fusion), kind=kCustom, calls=%fused_computation.3 | custom fusion | flops 524288 | bytes 6291520 | tf_op jit(solution)/shard_map/scatter-add | solution.py:64
  129.4 3.7 %fusion.3 = bf16[512,1024]{1,0:T(8,128)(2,1)S(1)} fusion(f32[16,32,1024]{2,1,0:T(8,128)} %scatter_fusion.1, f32[4,128,1024]{2,1,0:T(8,128)} %copy-done.1, f32[512,1024]{1,0:T(8,128)} %get-tuple-element.9, f32[1024]{0:T(1024)S(1)} %copy-done.7), kind=kLoop, calls=%fused_computation.16 | loop fusion | flops 2621440 | bytes 7344128 | tf_op jit(solution)/shard_map/convert_element_type | solution.py:68
  133.2 3.3 %convolution_bitcast_fusion = f32[1024,1024]{0,1:T(8,128)} fusion(bf16[512,1024]{1,0:T(8,128)(2,1)S(1)} %fusion.3, bf16[512,1024]{1,0:T(8,128)(2,1)S(1)} %copy-done.3), kind=kOutput, calls=%fused_computation.8 | convolution fusion | flops 1073741824 | bytes 6291456 | tf_op jit(solution)/shard_map/dot_general | solution.py:73
  136.4 5.3 %copy.35 = f32[1024,1024]{1,0:T(8,128)} copy(f32[1024,1024]{0,1:T(8,128)} %convolution_bitcast_fusion) | data formatting | bytes 8388608
  141.9 61.1 %reduce-scatter.4.cloned.1.call-done = f32[64,1024]{1,0:T(8,128)} async-done(((f32[1024,1024]{1,0:T(8,128)}), f32[64,1024]{1,0:T(8,128)}) %reduce-scatter.4.cloned.1.call-update) | async-done | bytes 262160 | tf_op jit(solution)/shard_map/reduce_scatter | solution.py:72
  203.0 2.3 convolution_convert_fusion
  205.3 103.8 %all-gather.3.cloned.1.call-done = f32[2048,1024]{1,0:T(8,128)} async-done(((f32[64,1024]{1,0:T(8,128)}), f32[2048,1024]{1,0:T(8,128)}) %all-gather.3.cloned.1.call-update) | async-done | bytes 8388624 | tf_op jit(solution)/shard_map/all_gather | solution.py:81
  309.1 4.0 %reduce_sum.49 = f32[64,1024]{1,0:T(8,128)S(1)} reduce(f32[32,64,1024]{2,1,0:T(8,128)} %bitcast.39, f32[]{:T(128)} %constant.22.clone.1), dimensions={0}, to_apply=%region_8.9 | reduce | flops 2031616 | bytes 8650756 | tf_op jit(solution)/shard_map/reduce_sum | solution.py:81
  (43 shorter events, 9.6 us)
Async XLA Ops:
  7.2 13.5 %copy-start = (bf16[1024,1024]{1,0:T(8,128)(2,1)S(1)}, bf16[1024,1024]{1,0:T(8,128)(2,1)}, u32[]{:S(2)}) copy-start(bf16[1024,1024]{1,0:T(8,128)(2,1)} %param.8) | copy-start | bytes 6291460
  8.8 18.8 %all-to-all-start = ((s32[16,1,1]{2,1,0:T(1,128)}), s32[16,1,1]{2,1,0:T(1,128)S(1)}, u32[]{:S(2)}, u32[]{:S(2)}) async-start(s32[16,1,1]{2,1,0:T(1,128)} %copy.29), calls=%async_computation | async-start | bytes 16384 | tf_op jit(solution)/shard_map/all_to_all | solution.py:35
  28.0 6.5 %copy-start.5 = (s32[512,16]{0,1:T(8,128)S(1)}, s32[512,16]{0,1:T(8,128)}, u32[]{:S(2)}) copy-start(s32[512,16]{0,1:T(8,128)} %param.12) | copy-start | bytes 98308
  28.0 6.6 %copy-start.6 = (s32[512,16]{0,1:T(8,128)S(1)}, s32[512,16]{0,1:T(8,128)}, u32[]{:S(2)}) copy-start(s32[512,16]{0,1:T(8,128)} %param.11) | copy-start | bytes 98308
  29.6 32.9 %all-to-all-start.1 = ((bf16[16,32,1024]{2,1,0:T(8,128)(2,1)}), bf16[16,32,1024]{2,1,0:T(8,128)(2,1)}, u32[]{:S(2)}, u32[]{:S(2)}) async-start(bf16[16,32,1024]{2,1,0:T(8,128)(2,1)} %gather_fusion), calls=%async_computation.1 | async-start | bytes 2097152 | tf_op jit(solution)/shard_map/all_to_all | solution.py:39
  68.8 2.6 copy-start.2
  71.9 1.4 copy-start.4
  73.3 2.8 copy-start.1
  91.2 31.5 %all-to-all-start.2 = ((bf16[16,32,1024]{2,1,0:T(8,128)(2,1)}), bf16[16,32,1024]{2,1,0:T(8,128)(2,1)S(1)}, u32[]{:S(2)}, u32[]{:S(2)}) async-start(bf16[16,32,1024]{2,1,0:T(8,128)(2,1)} %slice.16), calls=%async_computation.2 | async-start | bytes 2097152 | tf_op jit(solution)/shard_map/all_to_all | solution.py:62
  94.8 108.2 %reduce-scatter.4.cloned.1.call-start = ((), (), s32[]{:S(2)}) async-start(), calls=%async_computation.5 | async-start | bytes 4456448 | tf_op jit(solution)/shard_map/reduce_scatter | solution.py:72
  124.4 5.1 %copy-start.7 = (f32[1024]{0:T(1024)S(1)}, f32[1024]{0:T(1024)}, u32[]{:S(2)}) copy-start(f32[1024]{0:T(1024)} %param.9) | copy-start | bytes 12292
  129.4 3.7 %copy-start.3 = (bf16[512,1024]{1,0:T(8,128)(2,1)S(1)}, bf16[512,1024]{1,0:T(8,128)(2,1)}, u32[]{:S(2)}) copy-start(bf16[512,1024]{1,0:T(8,128)(2,1)} %param.7) | copy-start | bytes 3145732
  141.8 167.3 %all-gather.3.cloned.1.call-start = ((), (), s32[]{:S(2)}) async-start(), calls=%async_computation.4 | async-start | bytes 8650752 | tf_op jit(solution)/shard_map/all_gather | solution.py:81
Sparse Core Ops, SparseCore 0:
  141.9 61.0 reduce-scatter.3
  206.2 102.8 all-gather.2
